TPU v7x, 512 devices: a whole 4x8x8 slice. The times are simulated.
512 devices in a mesh: lon: 32 (over y, x), tm: 16 (over z, core).
Axes of the slice: x: 4, y: 8, z: 8, core: 2. Of those that a mesh axis runs over, the one named last changes fastest.
Arguments:
- anomalies: bfloat16 [4096, 8192], P('lon', 'tm'), may hold values from -200 to 200, as said below
- neighbor_ids: int32 [16, 3], replicated, may hold values from 0 to 15, as said below
- neighbor_counts: int32 [16], replicated, may hold values from 1 to 3
- lag_set: int32 [9], replicated, may hold values from 0 to 128, as said below
Outputs:
- network: float32 [4096, 6912], P(('lon', 'tm'))
Inputs may be any that keep to these rules, and one draw needn't show every extreme that they name: `neighbor_ids`: row b lists 3 distinct blocks, each within loop distance 2 of block b (b itself may appear); only the first neighbor_counts[b] slots are used. `lag_set`: 9 distinct lags. Real-valued anomalies; no point's series is constant.
All inputs are finite; a program needn't handle non-finite values.
Results may differ from a plain program's by a relative error of at most 0.0037.
Values may be sent and summed in bfloat16 or wider, within the bound.
No kernel may reach another device: no remote copies, remote signals or barrier semaphores. Data moves between devices by JAX's collectives and lax.ppermute only.
A program may use at most 64 MiB of HBM per device.

v0:
```python
import jax
import jax.numpy as jnp
from jax import lax
from jax.sharding import PartitionSpec as P

LMAX = 128
NLAG = 9
K_SLOTS = 3
REACH = 2


def joined(part, axis, combine):
    gathered = jax.tree.map(lambda a: lax.all_gather(a, axis), part)

    def take(source):
        return jax.tree.map(lambda a: lax.dynamic_index_in_dim(a, source, 0, False), gathered)

    return lax.fori_loop(
        1, lax.axis_size(axis), lambda source, state: combine(state, take(source)), take(0)
    )


def shifted(value, axis, by):
    size = lax.axis_size(axis)
    pairs = [(i, i + by) for i in range(size) if 0 <= i + by < size]
    return lax.ppermute(value, axis, pairs)


def from_partner(value, axis, stride):
    mask = 2**stride
    pairs = [(source, source ^ mask) for source in range(lax.axis_size(axis))]
    return lax.ppermute(value, axis, pairs)


def shifted_2(value, axis, by):
    size = lax.axis_size(axis)
    return lax.ppermute(value, axis, [(i, (i + by) % size) for i in range(size)])


def chan_merge(earlier, later):
    count_first, mean_first, square_first = earlier
    count_second, mean_second, square_second = later
    merged = count_first + count_second
    delta = mean_second - mean_first
    new_mean = mean_first + delta * (count_second / merged)
    new_square = (
        square_first + square_second + delta * delta * (count_first * count_second / merged)
    )
    return (merged, new_mean, new_square)


def left_operand(own_rows, lag_days, days_dev):
    return jnp.concatenate(
        [own_rows[:, :days_dev], lax.dynamic_slice_in_dim(own_rows, lag_days, days_dev, 1)], 1
    )


def right_product(left_side, columns, lag_days, days_dev):
    right_side = jnp.concatenate(
        [lax.dynamic_slice_in_dim(columns, lag_days, days_dev, 1), columns[:, :days_dev]], 1
    )
    return lax.dot_general(
        left_side, right_side, (((1,), (1,)), ((), ())), preferred_element_type=jnp.float32
    )


def local(anomalies, neighbor_ids, neighbor_counts, lag_set):
    half_rows, days_dev = anomalies.shape
    tm_size = lax.axis_size("tm")
    blocks = lax.axis_size("lon") // 2
    block_width = 2 * half_rows
    total_days = days_dev * tm_size
    values = anomalies.astype(jnp.float32)
    shard_mean = jnp.mean(values, axis=1)
    shard_square = jnp.sum(jnp.square(values - shard_mean[:, None]), axis=1)
    shard_count = jnp.full((1,), days_dev, jnp.float32)
    merged_count, point_mean, point_m2 = joined(
        (shard_count, shard_mean, shard_square), "tm", chan_merge
    )
    spread = jnp.sqrt(point_m2 / merged_count + 1e-06)
    standardized = ((values - point_mean[:, None]) / spread[:, None]).astype(jnp.bfloat16)
    margin = shifted(standardized[:, :LMAX], "tm", -1)
    extended = jnp.concatenate([standardized, margin], 1)
    partner = from_partner(extended, "lon", 0)
    lon_index = lax.axis_index("lon")
    parity = lon_index % 2
    own_block = jnp.where(
        parity == 0,
        jnp.concatenate([extended, partner], 0),
        jnp.concatenate([partner, extended], 0),
    )
    block_index = lon_index // 2
    later_blocks = []
    earlier_blocks = []
    for offset in range(1, REACH + 1):
        later_blocks.append(shifted_2(own_block, "lon", -2 * offset))
        earlier_blocks.append(shifted_2(own_block, "lon", 2 * offset))
    candidates = jnp.stack(earlier_blocks[::-1] + [own_block] + later_blocks, 0)
    block_ids = lax.dynamic_index_in_dim(neighbor_ids, block_index, 0, keepdims=False)
    live_count = lax.dynamic_index_in_dim(neighbor_counts, block_index, 0, keepdims=False)
    positions = (block_ids - block_index + REACH) % blocks

    def term_rows(row_count):
        slot_columns = [
            lax.dynamic_index_in_dim(candidates, positions[slot_index], 0, keepdims=False)
            for slot_index in range(K_SLOTS)
        ]
        by_slot = [[] for slot_index in range(K_SLOTS)]
        for lag_index in range(NLAG):
            left_side = left_operand(extended, lag_set[lag_index], days_dev)
            for slot_index in range(K_SLOTS):
                by_slot[slot_index].append(
                    right_product(left_side, slot_columns[slot_index], lag_set[lag_index], days_dev)
                )
        products = [item for slot_list in by_slot for item in slot_list]
        return jnp.stack(products, 1).reshape(row_count, -1)

    out_rows = half_rows // tm_size
    summed = lax.psum(term_rows(half_rows), "tm")
    comoment = lax.dynamic_slice_in_dim(summed, lax.axis_index("tm") * out_rows, out_rows, 0)
    comoment = comoment.reshape(out_rows, K_SLOTS, NLAG, block_width)
    denominator = 2.0 * (total_days - lag_set).astype(jnp.float32)
    is_live = jnp.arange(K_SLOTS, dtype=jnp.int32) < live_count
    linked = jnp.where(
        is_live[None, :, None, None], comoment / denominator[None, None, :, None], 0.0
    )
    squares = jnp.sum(jnp.square(linked), axis=(1, 2, 3))
    row_scale = jnp.sqrt(squares / (live_count * NLAG * block_width).astype(jnp.float32) + 1e-06)
    return (linked / row_scale[:, None, None, None]).reshape(out_rows, -1)


def solution(mesh):
    return jax.shard_map(
        local,
        mesh=mesh,
        in_specs=(P("lon", "tm"), P(), P(), P()),
        out_specs=P(("lon", "tm"), None),
        check_vma=False,
    )
```

profile of v0, /device:TPU:1, one launch (start us, length us, event | category | flops | bytes accessed | tf_op | source)
XLA Modules:
  0.0 342.7 jit_solution(14211399032186157105)
XLA Ops:
  6.5 1.3 dynamic-slice.54
  8.6 30.6 %all-reduce = f32[16]{0:T(128)S(1)} all-reduce(f32[16]{0:T(128)S(1)} %dynamic-update-slice), channel_id=1, replica_groups=mesh['lon'=32,'tm'=16] {'tm'}, use_global_device_ids=true, to_apply=%add | all-reduce | flops 16 | bytes 128
  40.2 1.1 fusion.61
  41.3 16.8 %all-gather.3 = f32[16,1,128]{2,1,0:T(1,128)S(1)} all-gather(f32[1,1,128]{2,1,0:T(1,128)S(1)} %bitcast.237), channel_id=3, replica_groups=mesh['lon'=32,'tm'=16] {'tm'}, dimensions={0}, use_global_device_ids=true | all-gather | bytes 8704 | tf_op jit(solution)/shard_map/all_gather | solution.py:13
  58.1 16.0 %all-gather.2 = f32[16,1,128]{2,1,0:T(1,128)S(1)} all-gather(f32[1,1,128]{2,1,0:T(1,128)S(1)} %get-tuple-element.256), channel_id=2, replica_groups=mesh['lon'=32,'tm'=16] {'tm'}, dimensions={0}, use_global_device_ids=true | all-gather | bytes 8704 | tf_op jit(solution)/shard_map/all_gather | solution.py:13
  74.1 39.3 %while.19 = (s32[]{:T(128)}, f32[1]{0:T(128)}, f32[128]{0:T(128)S(1)}, f32[128]{0:T(128)S(1)}, f32[16,1]{0,1:T(1,128)S(1)}, /*index=5*/f32[16,128]{1,0:T(8,128)S...) while((s32[]{:T(128)}, f32[1]{0:T(128)}, f32[128]{0:T(128)S(1)}, f32[128]{0:T(128)S(1)}, ...), condition=%wide.region_3.4_spmd, body=%wide.region_2.3_spmd.sunk | while | flops 905 | bytes 3295 | solution.py:18
  113.4 1.0 fusion.63
  114.4 2.1 collective-permute-start
  117.4 2.2 collective-permute-done
  119.7 3.1 collective-permute-start.1
  127.3 3.2 collective-permute-start.2
  130.5 1.7 fusion.107
  151.5 4.4 %collective-permute-start.3 = (bf16[256,640]{1,0:T(8,128)(2,1)S(1)}, bf16[256,640]{1,0:T(8,128)(2,1)S(1)}, u32[]{:S(2)}, u32[]{:S(2)}) collective-permute-start(bf16[256,640]{1,0:T(8,128)(2,1)S(1)} %maximum_select_fusion), channel_id=1, source_target_pairs={{0,32},{16,48},{32,64},{48,80},{64,96},{80,112},{96,128},{112,144}... | collective-permute-start | bytes 983048 | tf_op jit(solution)/shard_map/ppermute | solution.py:37
  156.2 4.5 %collective-permute-start.4 = (bf16[256,640]{1,0:T(8,128)(2,1)S(1)}, bf16[256,640]{1,0:T(8,128)(2,1)S(1)}, u32[]{:S(2)}, u32[]{:S(2)}) collective-permute-start(bf16[256,640]{1,0:T(8,128)(2,1)S(1)} %maximum_select_fusion), channel_id=1, source_target_pairs={{0,480},{16,496},{32,0},{48,16},{64,32},{80,48},{96,64},{112,80},{... | collective-permute-start | bytes 983048 | tf_op jit(solution)/shard_map/ppermute | solution.py:37
  160.7 2.8 collective-permute-start.5
  163.6 5.9 %collective-permute-done.3 = bf16[256,640]{1,0:T(8,128)(2,1)S(1)} collective-permute-done((bf16[256,640]{1,0:T(8,128)(2,1)S(1)}, bf16[256,640]{1,0:T(8,128)(2,1)S(1)}, u32[]{:S(2)}, u32[]{:S(2)}) %collective-permute-start.3) | collective-permute-done | bytes 327712 | tf_op jit(solution)/shard_map/ppermute | solution.py:37
  169.6 3.2 collective-permute-done.4
  172.8 2.4 collective-permute-done.5
  175.4 4.5 %dynamic-slice_bitcast_fusion.3 = (bf16[256,512]{1,0:T(8,128)(2,1)S(1)}, bf16[256,512]{1,0:T(8,128)(2,1)S(1)}, bf16[256,512]{1,0:T(8,128)(2,1)S(1)}, bf16[256,51...) fusion(bf16[5,256,640]{2,1,0:T(8,128)(2,1)S(1)} %bitcast_dynami, ...), kind=kLoop, calls=%fused_computation.153 | loop fusion | bytes 14155824 | tf_op jit(solution)/shard_map/dynamic_slice | solution.py:60
  205.8 3.3 copy.9
  209.1 3.0 copy.10
  214.8 118.2 %all-reduce.3.cloned.1.call-done = f32[128,6912]{1,0:T(8,128)} async-done(((f32[128,6912]{1,0:T(8,128)}), f32[128,6912]{1,0:T(8,128)}) %all-reduce.3.cloned.1.call-update) | async-done | bytes 3538960 | tf_op jit(solution)/shard_map/psum | solution.py:119
  333.0 1.1 multiply_reduce_fusion
  334.2 1.7 broadcast_divide_fusion
  (97 shorter events, 41.8 us)
Async XLA Ops:
  6.5 326.5 %all-reduce.3.cloned.1.call-start = ((), (), s32[]{:S(2)}) async-start(), calls=%async_computation | async-start | bytes 7077888 | tf_op jit(solution)/shard_map/psum | solution.py:119
  114.4 5.2 %collective-permute-start = (bf16[128,128]{1,0:T(8,128)(2,1)S(1)}, bf16[128,128]{1,0:T(8,128)(2,1)S(1)}, u32[]{:S(2)}, u32[]{:S(2)}) collective-permute-start(bf16[128,128]{1,0:T(8,128)(2,1)S(1)} %slice.58), channel_id=1, source_target_pairs={{1,0},{2,1},{3,2},{4,3},{5,4},{6,5},{7,6},{8,7},{9,8},{10,9},{11,1... | collective-permute-start | bytes 98312 | tf_op jit(solution)/shard_map/ppermute | solution.py:26
  119.7 7.5 %collective-permute-start.1 = (bf16[128,640]{1,0:T(8,128)(2,1)S(1)}, bf16[128,640]{1,0:T(8,128)(2,1)S(1)}, u32[]{:S(2)}, u32[]{:S(2)}) collective-permute-start(bf16[128,640]{1,0:T(8,128)(2,1)S(1)} %get-tuple-element.242), channel_id=1, source_target_pairs={{0,16},{16,0},{32,48},{48,32},{64,80},{80,64},{96,112},{112,96},{1... | collective-permute-start | bytes 491528 | tf_op jit(solution)/shard_map/ppermute | solution.py:32
  127.3 36.2 %collective-permute-start.2 = (bf16[256,640]{1,0:T(8,128)(2,1)S(1)}, bf16[256,640]{1,0:T(8,128)(2,1)S(1)}, u32[]{:S(2)}, u32[]{:S(2)}) collective-permute-start(bf16[256,640]{1,0:T(8,128)(2,1)S(1)} %maximum_select_fusion), channel_id=1, source_target_pairs={{0,64},{16,80},{32,96},{48,112},{64,128},{80,144},{96,160},{112,17... | collective-permute-start | bytes 983048 | tf_op jit(solution)/shard_map/ppermute | solution.py:37
  151.5 18.0 %collective-permute-start.3 = (bf16[256,640]{1,0:T(8,128)(2,1)S(1)}, bf16[256,640]{1,0:T(8,128)(2,1)S(1)}, u32[]{:S(2)}, u32[]{:S(2)}) collective-permute-start(bf16[256,640]{1,0:T(8,128)(2,1)S(1)} %maximum_select_fusion), channel_id=1, source_target_pairs={{0,32},{16,48},{32,64},{48,80},{64,96},{80,112},{96,128},{112,144}... | collective-permute-start | bytes 983048 | tf_op jit(solution)/shard_map/ppermute | solution.py:37
  156.2 16.6 %collective-permute-start.4 = (bf16[256,640]{1,0:T(8,128)(2,1)S(1)}, bf16[256,640]{1,0:T(8,128)(2,1)S(1)}, u32[]{:S(2)}, u32[]{:S(2)}) collective-permute-start(bf16[256,640]{1,0:T(8,128)(2,1)S(1)} %maximum_select_fusion), channel_id=1, source_target_pairs={{0,480},{16,496},{32,0},{48,16},{64,32},{80,48},{96,64},{112,80},{... | collective-permute-start | bytes 983048 | tf_op jit(solution)/shard_map/ppermute | solution.py:37
  160.7 14.5 %collective-permute-start.5 = (bf16[256,640]{1,0:T(8,128)(2,1)S(1)}, bf16[256,640]{1,0:T(8,128)(2,1)S(1)}, u32[]{:S(2)}, u32[]{:S(2)}) collective-permute-start(bf16[256,640]{1,0:T(8,128)(2,1)S(1)} %maximum_select_fusion), channel_id=1, source_target_pairs={{0,448},{16,464},{32,480},{48,496},{64,0},{80,16},{96,32},{112,48}... | collective-permute-start | bytes 983048 | tf_op jit(solution)/shard_map/ppermute | solution.py:37
  212.1 0.7 copy-start.1
  212.1 2.0 copy-start
Sparse Core Ops, SparseCore 0:
  212.2 120.7 all-reduce.2
where the time goes:
time: 344 us; the launch traced here: 343 us
  waiting for transfers between devices  132 us (38%)
  blocking collectives  63.3 us (18%)
  between operations  36.7 us (11%)
  loops' own time  30.2 us (9%)
  matrix products  25.8 us (8%)
  local copies, waits for them, and re-layouts  25.6 us (7%)
  starting transfers between devices  20.1 us (6%)
  other arithmetic  9.1 us (3%)
    psum x1, waiting for transfers between devices, local(): summed = lax.psum(term_rows(half_rows), 'tm')  118 us
    all_gather x2, blocking collectives, joined(): gathered = jax.tree.map(lambda a: lax.all_gather(a, axis), part)  32.7 us
    unnamed x1, blocking collectives  30.6 us
    another operation x1, loops' own time, joined(): lax.fori_loop(1, lax.axis_size(axis), lambda source, state: combine(state...  30.2 us
    dot_general x27, matrix products, right_product(): lax.dot_general(left_side, right_side, (((1,), (1,)), ((), ())), preferre...  25.8 us
    ppermute x4, starting transfers between devices, shifted_2(): lax.ppermute(value, axis, [(i, (i + by) % size) for i in range(size)])  14.9 us
    ppermute x4, waiting for transfers between devices, shifted_2(): lax.ppermute(value, axis, [(i, (i + by) % size) for i in range(size)])  11.5 us
    dynamic_slice x17, local copies, waits for them, and re-layouts, take(): lax.dynamic_index_in_dim(a, source, 0, False)  8.78 us
  transfers between devices with their start and end apart: 7, of which 5 were waited for; matrix products, arithmetic and copies ran while one was open for 2% of the time, Pallas kernels for 0%

commit v1 on v0

--- a/solution.py
+++ b/solution.py
@@ -116,7 +116,9 @@
         return jnp.stack(products, 1).reshape(row_count, -1)
 
     out_rows = half_rows // tm_size
-    summed = lax.psum(term_rows(half_rows), "tm")
+    x = term_rows(half_rows)
+    parts = lax.all_gather(x, "tm")
+    summed = jnp.sum(parts, axis=0)
     comoment = lax.dynamic_slice_in_dim(summed, lax.axis_index("tm") * out_rows, out_rows, 0)
     comoment = comoment.reshape(out_rows, K_SLOTS, NLAG, block_width)
     denominator = 2.0 * (total_days - lag_set).astype(jnp.float32)

time: 344 us -> 524 us (1.52)
  waiting for transfers between devices: 132 us -> 293 us
  other arithmetic: 9.1 us -> 26.9 us
    all_gather x0 -> x1, waiting for transfers between devices: none -> 279 us  [local(): parts = lax.all_gather(x, 'tm')]
    psum x1 -> x0, waiting for transfers between devices: 118 us -> none  [local(): summed = lax.psum(term_rows(half_rows), 'tm')]
    reduce_sum x0 -> x1, other arithmetic: none -> 18.2 us  [local(): summed = jnp.sum(parts, axis=0)]
  transfers between devices with their start and end apart: 7 -> 7, of which waited for: 5 -> 5; matrix products, arithmetic and copies ran while one was open for 2% -> 1% of each run, Pallas kernels for 0% -> 0%
where the time goes in v1:
time: 524 us; the launch traced here: 522 us
  waiting for transfers between devices  293 us (56%)
  blocking collectives  63.3 us (12%)
  between operations  36.7 us (7%)
  loops' own time  30.2 us (6%)
  other arithmetic  26.9 us (5%)
  local copies, waits for them, and re-layouts  26.2 us (5%)
  matrix products  25.8 us (5%)
  starting transfers between devices  20.1 us (4%)
    all_gather x1, waiting for transfers between devices, local(): parts = lax.all_gather(x, 'tm')  279 us
    all_gather x2, blocking collectives, joined(): gathered = jax.tree.map(lambda a: lax.all_gather(a, axis), part)  32.7 us
    unnamed x1, blocking collectives  30.6 us
    another operation x1, loops' own time, joined(): lax.fori_loop(1, lax.axis_size(axis), lambda source, state: combine(state...  30.2 us
    dot_general x27, matrix products, right_product(): lax.dot_general(left_side, right_side, (((1,), (1,)), ((), ())), preferre...  25.8 us
    reduce_sum x1, other arithmetic, local(): summed = jnp.sum(parts, axis=0)  18.2 us
    ppermute x4, starting transfers between devices, shifted_2(): lax.ppermute(value, axis, [(i, (i + by) % size) for i in range(size)])  14.9 us
    ppermute x4, waiting for transfers between devices, shifted_2(): lax.ppermute(value, axis, [(i, (i + by) % size) for i in range(size)])  11.5 us
  transfers between devices with their start and end apart: 7, of which 5 were waited for; matrix products, arithmetic and copies ran while one was open for 1% of the time, Pallas kernels for 0%

profile of v1, /device:TPU:1, one launch (start us, length us, event | category | flops | bytes accessed | tf_op | source)
XLA Modules:
  0.0 522.3 jit_solution(4495334665383964731)
XLA Ops:
  6.5 1.3 dynamic-slice.54
  8.6 30.6 %all-reduce = f32[16]{0:T(128)S(1)} all-reduce(f32[16]{0:T(128)S(1)} %dynamic-update-slice), channel_id=1, replica_groups=mesh['lon'=32,'tm'=16] {'tm'}, use_global_device_ids=true, to_apply=%add | all-reduce | flops 16 | bytes 128
  40.2 1.1 fusion.61
  41.3 16.8 %all-gather.3 = f32[16,1,128]{2,1,0:T(1,128)S(1)} all-gather(f32[1,1,128]{2,1,0:T(1,128)S(1)} %bitcast.237), channel_id=3, replica_groups=mesh['lon'=32,'tm'=16] {'tm'}, dimensions={0}, use_global_device_ids=true | all-gather | bytes 8704 | tf_op jit(solution)/shard_map/all_gather | solution.py:13
  58.1 16.0 %all-gather.2 = f32[16,1,128]{2,1,0:T(1,128)S(1)} all-gather(f32[1,1,128]{2,1,0:T(1,128)S(1)} %get-tuple-element.256), channel_id=2, replica_groups=mesh['lon'=32,'tm'=16] {'tm'}, dimensions={0}, use_global_device_ids=true | all-gather | bytes 8704 | tf_op jit(solution)/shard_map/all_gather | solution.py:13
  74.1 39.3 %while.19 = (s32[]{:T(128)}, f32[1]{0:T(128)}, f32[128]{0:T(128)S(1)}, f32[128]{0:T(128)S(1)}, f32[16,1]{0,1:T(1,128)S(1)}, /*index=5*/f32[16,128]{1,0:T(8,128)S...) while((s32[]{:T(128)}, f32[1]{0:T(128)}, f32[128]{0:T(128)S(1)}, f32[128]{0:T(128)S(1)}, ...), condition=%wide.region_3.4_spmd, body=%wide.region_2.3_spmd.sunk | while | flops 905 | bytes 3295 | solution.py:18
  113.4 1.0 fusion.63
  114.4 2.1 collective-permute-start
  117.4 2.2 collective-permute-done
  119.7 3.1 collective-permute-start.1
  127.3 3.2 collective-permute-start.2
  130.5 1.7 fusion.107
  151.5 4.4 collective-permute-start.3
  156.2 4.5 collective-permute-start.4
  160.7 2.8 collective-permute-start.5
  163.6 5.9 %collective-permute-done.3 = bf16[256,640]{1,0:T(8,128)(2,1)S(1)} collective-permute-done((bf16[256,640]{1,0:T(8,128)(2,1)S(1)}, bf16[256,640]{1,0:T(8,128)(2,1)S(1)}, u32[]{:S(2)}, u32[]{:S(2)}) %collective-permute-start.3) | collective-permute-done | bytes 327712 | tf_op jit(solution)/shard_map/ppermute | solution.py:37
  169.6 3.2 collective-permute-done.4
  172.8 2.4 collective-permute-done.5
  175.4 4.5 dynamic-slice_bitcast_fusion.3
  205.8 3.3 copy.10
  209.1 3.0 copy.11
  215.5 279.3 %all-gather.6.cloned.1.call-done = f32[16,128,6912]{2,1,0:T(8,128)} async-done(((f32[1,128,6912]{2,1,0:T(8,128)}), f32[16,128,6912]{2,1,0:T(8,128)}) %all-gather.6.cloned.1.call-update) | async-done | bytes 56623120 | tf_op jit(solution)/shard_map/all_gather | solution.py:120
  494.8 18.2 %reduce_sum.38 = f32[128,6912]{1,0:T(8,128)S(1)} reduce(f32[16,128,6912]{2,1,0:T(8,128)} %all-gather.6.cloned.1.call-done, f32[]{:T(128)} %constant.560.clone.1), dimensions={0}, to_apply=%region_4.5 | reduce | flops 13271040 | bytes 60162052 | tf_op jit(solution)/shard_map/reduce_sum | solution.py:121
  513.9 1.5 broadcast_divide_fusion
  (98 shorter events, 43.3 us)
Async XLA Ops:
  6.5 488.3 %all-gather.6.cloned.1.call-start = ((), (), s32[]{:S(2)}) async-start(), calls=%async_computation | async-start | bytes 60162048 | tf_op jit(solution)/shard_map/all_gather | solution.py:120
  114.4 5.2 %collective-permute-start = (bf16[128,128]{1,0:T(8,128)(2,1)S(1)}, bf16[128,128]{1,0:T(8,128)(2,1)S(1)}, u32[]{:S(2)}, u32[]{:S(2)}) collective-permute-start(bf16[128,128]{1,0:T(8,128)(2,1)S(1)} %slice.58), channel_id=1, source_target_pairs={{1,0},{2,1},{3,2},{4,3},{5,4},{6,5},{7,6},{8,7},{9,8},{10,9},{11,1... | collective-permute-start | bytes 98312 | tf_op jit(solution)/shard_map/ppermute | solution.py:26
  119.7 7.5 %collective-permute-start.1 = (bf16[128,640]{1,0:T(8,128)(2,1)S(1)}, bf16[128,640]{1,0:T(8,128)(2,1)S(1)}, u32[]{:S(2)}, u32[]{:S(2)}) collective-permute-start(bf16[128,640]{1,0:T(8,128)(2,1)S(1)} %get-tuple-element.242), channel_id=1, source_target_pairs={{0,16},{16,0},{32,48},{48,32},{64,80},{80,64},{96,112},{112,96},{1... | collective-permute-start | bytes 491528 | tf_op jit(solution)/shard_map/ppermute | solution.py:32
  127.3 36.2 %collective-permute-start.2 = (bf16[256,640]{1,0:T(8,128)(2,1)S(1)}, bf16[256,640]{1,0:T(8,128)(2,1)S(1)}, u32[]{:S(2)}, u32[]{:S(2)}) collective-permute-start(bf16[256,640]{1,0:T(8,128)(2,1)S(1)} %maximum_select_fusion), channel_id=1, source_target_pairs={{0,64},{16,80},{32,96},{48,112},{64,128},{80,144},{96,160},{112,17... | collective-permute-start | bytes 983048 | tf_op jit(solution)/shard_map/ppermute | solution.py:37
  151.5 18.0 %collective-permute-start.3 = (bf16[256,640]{1,0:T(8,128)(2,1)S(1)}, bf16[256,640]{1,0:T(8,128)(2,1)S(1)}, u32[]{:S(2)}, u32[]{:S(2)}) collective-permute-start(bf16[256,640]{1,0:T(8,128)(2,1)S(1)} %maximum_select_fusion), channel_id=1, source_target_pairs={{0,32},{16,48},{32,64},{48,80},{64,96},{80,112},{96,128},{112,144}... | collective-permute-start | bytes 983048 | tf_op jit(solution)/shard_map/ppermute | solution.py:37
  156.2 16.6 %collective-permute-start.4 = (bf16[256,640]{1,0:T(8,128)(2,1)S(1)}, bf16[256,640]{1,0:T(8,128)(2,1)S(1)}, u32[]{:S(2)}, u32[]{:S(2)}) collective-permute-start(bf16[256,640]{1,0:T(8,128)(2,1)S(1)} %maximum_select_fusion), channel_id=1, source_target_pairs={{0,480},{16,496},{32,0},{48,16},{64,32},{80,48},{96,64},{112,80},{... | collective-permute-start | bytes 983048 | tf_op jit(solution)/shard_map/ppermute | solution.py:37
  160.7 14.5 %collective-permute-start.5 = (bf16[256,640]{1,0:T(8,128)(2,1)S(1)}, bf16[256,640]{1,0:T(8,128)(2,1)S(1)}, u32[]{:S(2)}, u32[]{:S(2)}) collective-permute-start(bf16[256,640]{1,0:T(8,128)(2,1)S(1)} %maximum_select_fusion), channel_id=1, source_target_pairs={{0,448},{16,464},{32,480},{48,496},{64,0},{80,16},{96,32},{112,48}... | collective-permute-start | bytes 983048 | tf_op jit(solution)/shard_map/ppermute | solution.py:37
  212.1 0.7 copy-start.1
  212.1 2.0 copy-start
Sparse Core Ops, SparseCore 0:
  212.3 282.4 all-gather.5
